TPU v7x, 512 devices: a whole 4x4x16 slice. The times are simulated.
512 devices in a mesh: fsdp: 128 (over z, y, core), seq: 4 (over x).
Axes of the slice: x: 4, y: 4, z: 16, core: 2. Of those that a mesh axis runs over, the one named last changes fastest.
Arguments:
- tokens: bfloat16 [128, 512, 8192], P('fsdp', 'seq'), may hold values from -6 to 6
- queries: bfloat16 [128, 512, 8192], P('fsdp', None, 'seq'), may hold values from -6 to 6
- key_weight: bfloat16 [8192, 1024], P('fsdp', 'seq'), may hold values from -1 to 1
- u_factor: float32 [8192, 64], P('fsdp'), may hold values from -6 to 6
- v_factor: float32 [1024, 64], replicated, may hold values from -6 to 6
Outputs:
- update: float32 [8192, 1024], P('fsdp')
- losses: float32 [2], replicated
All inputs are finite; a program needn't handle non-finite values.
Results may differ from a plain program's by a relative error of at most 0.0003.
Values may be sent and summed in bfloat16 or wider, within the bound.
No kernel may reach another device: no remote copies, remote signals or barrier semaphores. Data moves between devices by JAX's collectives and lax.ppermute only.
A program may use at most 64 MiB of HBM per device.

v0:
```python
import math
import jax
import jax.numpy as jnp
from jax import lax
from jax.sharding import PartitionSpec as P

D = 8192
HQ = 64
HD = 128
R = 64
KD = 1024
GROUP = 8


def highest(left, right):
    return jnp.dot(left, right, precision=lax.Precision.HIGHEST, preferred_element_type=jnp.float32)


def solve_rows(rows, gram):
    lower = jnp.linalg.cholesky(gram)
    return lax.linalg.triangular_solve(lower, rows, left_side=False, lower=True, transpose_a=True)


def local(tokens, queries, key_weight, u_factor, v_factor):
    q_v = v_factor
    for turn in range(2):
        q_v = solve_rows(q_v, highest(q_v.T, q_v))
    u_rows = u_factor
    for turn in range(2):
        whole_u = lax.all_gather(u_rows, "fsdp", axis=0, tiled=True)
        u_rows = solve_rows(u_rows, highest(whole_u.T, whole_u))
    q_low = u_rows.astype(jnp.bfloat16)
    whole_x = lax.all_gather(tokens, "seq", axis=1, tiled=True)[0]
    length = whole_x.shape[0]
    slice_width = key_weight.shape[1]
    weight_piece = lax.all_gather(key_weight, "fsdp", axis=0, tiled=True)
    factor_piece = lax.all_gather(q_low, "fsdp", axis=0, tiled=True)
    base = jnp.dot(whole_x, weight_piece, preferred_element_type=jnp.float32)
    side = jnp.dot(whole_x, factor_piece, preferred_element_type=jnp.float32)
    col_start = lax.axis_index("seq") * slice_width
    v_slice = lax.dynamic_slice_in_dim(q_v, col_start, slice_width, 0)
    offset = 2.0 * highest(side, v_slice.T)
    keys = jnp.stack([base + offset, base - offset]).astype(jnp.bfloat16)
    local_kv = slice_width // HD
    query_rows = queries[0]
    query_heads = query_rows.reshape(length, local_kv, GROUP, HD).transpose(1, 2, 0, 3)
    key_heads = keys.reshape(2, length, local_kv, HD).transpose(2, 0, 1, 3)
    places = jnp.arange(length)
    causal = places[:, None] >= places[None, :]
    factor_scale = 1.0 / math.sqrt(HD)

    def one_query_head(query_one, key_one):
        scores = (
            jnp.einsum("td,npd->ntp", query_one, key_one, preferred_element_type=jnp.float32)
            * factor_scale
        )
        scores = jnp.where(causal[None], scores, -1e30)
        top = jnp.max(scores, axis=-1)
        total = jnp.sum(jnp.where(causal[None], jnp.exp(scores - top[..., None]), 0.0), axis=-1)
        return jnp.sum(top + jnp.log(total), axis=1)

    def one_key_head(pair):
        group_queries, key_one = pair
        return jnp.sum(
            lax.map(lambda query_one: one_query_head(query_one, key_one), group_queries), axis=0
        )

    partial_sums = jnp.sum(lax.map(one_key_head, (query_heads, key_heads)), axis=0)
    sums = lax.psum(partial_sums, ("fsdp", "seq"))
    losses = sums / (lax.axis_size("fsdp") * length * HQ)
    unit = math.sqrt(D * KD / R)
    update = unit * highest(u_rows, q_v.T)
    return (update, losses)


def solution(mesh):
    in_specs = (
        P("fsdp", "seq", None),
        P("fsdp", None, "seq"),
        P("fsdp", "seq"),
        P("fsdp", None),
        P(),
    )
    out_specs = (P("fsdp", None), P())
    return jax.shard_map(local, mesh=mesh, in_specs=in_specs, out_specs=out_specs, check_vma=False)
```

profile of v0, /device:TPU:1, one launch (start us, length us, event | category | flops | bytes accessed | tf_op | source)
XLA Modules:
  0.0 858.6 jit_solution(16340279235827252313)
XLA Ops:
  7.2 0.7 all-gather.6.cloned.1.call-update
  8.0 151.0 %all-gather.6.cloned.1.call-done = f32[8192,64]{1,0:T(8,128)} async-done(((f32[64,64]{1,0:T(8,128)}), f32[8192,64]{1,0:T(8,128)}) %all-gather.6.cloned.1.call-update) | async-done | bytes 2097168 | tf_op jit(solution)/shard_map/all_gather | solution.py:30
  159.0 10.4 %fusion.30 = f32[64,64]{1,0:T(8,128)S(1)} fusion(f32[8192,64]{1,0:T(8,128)} %all-gather.6.cloned.1.call-done), kind=kOutput, calls=%fused_computation.63 | convolution fusion | flops 402653184 | bytes 2113536 | tf_op jit(solution)/shard_map/dot_general | solution.py:16
  169.5 5.8 cholesky.74
  176.1 0.7 fusion.14
  176.7 4.9 custom-call.10
  181.9 0.7 copy.22
  182.8 137.7 %all-gather.8.cloned.1.call-done = f32[8192,64]{1,0:T(8,128)} async-done(((f32[64,64]{1,0:T(8,128)}), f32[8192,64]{1,0:T(8,128)}) %all-gather.8.cloned.1.call-update) | async-done | bytes 2097168 | tf_op jit(solution)/shard_map/all_gather | solution.py:30
  320.6 10.4 %fusion.31 = f32[64,64]{1,0:T(8,128)S(1)} fusion(f32[8192,64]{1,0:T(8,128)} %all-gather.8.cloned.1.call-done), kind=kOutput, calls=%fused_computation.64 | convolution fusion | flops 402653184 | bytes 2113536 | tf_op jit(solution)/shard_map/dot_general | solution.py:16
  331.1 5.8 cholesky.85
  337.6 0.7 fusion.15
  338.3 4.9 custom-call.11
  343.4 0.7 copy.27
  345.8 5.8 cholesky.96
  353.0 4.9 custom-call.12
  358.8 5.9 cholesky.107
  366.0 4.9 custom-call.13
  370.9 2.8 copy.26
  374.1 107.1 %all-gather.14.cloned.1.call-done = bf16[8192,64]{1,0:T(8,128)(2,1)} async-done(((bf16[64,64]{1,0:T(8,128)(2,1)}), bf16[8192,64]{1,0:T(8,128)(2,1)}) %all-gather.14.cloned.1.call-update) | async-done | bytes 1048592 | tf_op jit(solution)/shard_map/all_gather | solution.py:37
  481.1 88.4 %all-gather.10.cloned.1.call-done = bf16[1,512,8192]{2,1,0:T(8,128)(2,1)} async-done(((bf16[1,128,8192]{2,1,0:T(8,128)(2,1)}), bf16[1,512,8192]{2,1,0:T(8,128)(2,1)}) %all-gather.10.cloned.1.call-update) | async-done | bytes 8388624 | tf_op jit(solution)/shard_map/all_gather | solution.py:33
  569.6 6.7 fusion.9
  576.9 139.4 %all-gather.12.cloned.1.call-done = bf16[8192,256]{1,0:T(8,128)(2,1)} async-done(((bf16[64,256]{1,0:T(8,128)(2,1)}), bf16[8192,256]{1,0:T(8,128)(2,1)}) %all-gather.12.cloned.1.call-update) | async-done | bytes 4194320 | tf_op jit(solution)/shard_map/all_gather | solution.py:36
  716.3 6.9 add_convert_fusion
  723.7 25.3 %while.26 = (s32[]{:T(128)}, f32[2,2]{1,0:T(2,128)S(1)}, bf16[2,8,512,128]{2,3,1,0:T(8,128)(2,1)}, bf16[2,2,512,128]{3,2,1,0:T(8,128)(2,1)S(1)}, s32[]{:T(128)},...) while((s32[]{:T(128)}, f32[2,2]{1,0:T(2,128)S(1)}, ...), condition=%wide.region_9.13_spmd.clone.clone, body=%wide.region_2.12_spmd.clone.clone.sunk | while | flops 138674192 | bytes 10113394 | solution.py:68
  723.7 1.3 constant_dynamic-slice_fusion.2
  725.0 0.7 copy.33
  725.8 10.4 %while.27 = (s32[]{:T(128)}, f32[8,2]{1,0:T(8,128)S(1)}, pred[512,512]{0,1:T(8,128)(4,1)S(1)}, bf16[8,512,128]{2,1,0:T(8,128)(2,1)S(1)}, bf16[2,512,128]{2,1,0:T(8,128)(2,1)S(1)}, /*index=5*/s32[]{:T(128)}, s32[]{:T(128)}) while((s32[]{:T(128)}, f32[8,2]{1,0:T(8,128)S(1)}, pred[512,512]{0,1:T(8,128)(4,1)S(1)}, ...), condition=%wide.region_7.10_spmd.clone, body=%wide.region_3.9_spmd.clone.sunk | while | flops 138412032 | bytes 5132397 | solution.py:65
  736.3 1.3 constant_dynamic-slice_fusion.2
  737.7 0.7 copy.33
  738.5 10.4 %while.27 = (s32[]{:T(128)}, f32[8,2]{1,0:T(8,128)S(1)}, pred[512,512]{0,1:T(8,128)(4,1)S(1)}, bf16[8,512,128]{2,1,0:T(8,128)(2,1)S(1)}, bf16[2,512,128]{2,1,0:T(8,128)(2,1)S(1)}, /*index=5*/s32[]{:T(128)}, s32[]{:T(128)}) while((s32[]{:T(128)}, f32[8,2]{1,0:T(8,128)S(1)}, pred[512,512]{0,1:T(8,128)(4,1)S(1)}, ...), condition=%wide.region_7.10_spmd.clone, body=%wide.region_3.9_spmd.clone.sunk | while | flops 138412032 | bytes 5132397 | solution.py:65
  749.0 1.1 convolution_multiply_fusion.1
  750.1 101.5 %psum.7 = f32[2]{0:T(128)S(1)} all-reduce(f32[2]{0:T(128)S(1)} %reduce_sum.36), channel_id=1, replica_groups=mesh['fsdp'=128,'seq'=4] {'fsdp','seq'}, use_global_device_ids=true, to_apply=%region_11.15 | all-reduce | flops 2 | bytes 16 | tf_op jit(solution)/shard_map/psum | solution.py:69
  (120 shorter events, 30.4 us)
Async XLA Ops:
  7.2 338.2 %copy-start = (f32[1024,64]{0,1:T(8,128)S(1)}, f32[1024,64]{0,1:T(8,128)}, u32[]{:S(2)}) copy-start(f32[1024,64]{0,1:T(8,128)} %param.18) | copy-start | bytes 786436
  7.2 151.8 %all-gather.6.cloned.1.call-start = ((), (), s32[]{:S(2)}) async-start(), calls=%async_computation | async-start | bytes 4227072 | tf_op jit(solution)/shard_map/all_gather | solution.py:30
  7.9 173.7 %copy-start.2 = (f32[64,64]{1,0:T(8,128)S(1)}, f32[64,64]{1,0:T(8,128)}, u32[]{:S(2)}) copy-start(f32[64,64]{1,0:T(8,128)} %param.17) | copy-start | bytes 49156
  7.9 312.6 %all-gather.8.cloned.1.call-start = ((), (), s32[]{:S(2)}) async-start(), calls=%async_computation.1 | async-start | bytes 4227072 | tf_op jit(solution)/shard_map/all_gather | solution.py:30
  182.6 298.5 %all-gather.14.cloned.1.call-start = ((), (), s32[]{:S(2)}) async-start(), calls=%async_computation.4 | async-start | bytes 2113536 | tf_op jit(solution)/shard_map/all_gather | solution.py:37
  344.2 26.7 %copy-start.1 = (bf16[1,512,2048]{2,1,0:T(8,128)(2,1)S(1)}, bf16[1,512,2048]{2,1,0:T(8,128)(2,1)}, u32[]{:S(2)}) copy-start(bf16[1,512,2048]{2,1,0:T(8,128)(2,1)} %param.15) | copy-start | bytes 6291460
  344.2 225.4 %all-gather.10.cloned.1.call-start = ((), (), s32[]{:S(2)}) async-start(), calls=%async_computation.2 | async-start | bytes 10485760 | tf_op jit(solution)/shard_map/all_gather | solution.py:33
  344.7 371.6 %all-gather.12.cloned.1.call-start = ((), (), s32[]{:S(2)}) async-start(), calls=%async_computation.3 | async-start | bytes 4227072 | tf_op jit(solution)/shard_map/all_gather | solution.py:36
Sparse Core Ops, SparseCore 0:
  11.1 147.8 all-gather.5
  182.7 137.7 all-gather.7
  344.3 136.8 all-gather.13
  483.1 86.4 all-gather.9
  572.5 143.6 all-gather.11
where the time goes:
time: 859 us
  waiting for transfers between devices  625 us (73%)
  blocking collectives  101 us (12%)
  other arithmetic  60.3 us (7%)
  matrix products  47.2 us (5%)
  between operations  14 us (2%)
  local copies, waits for them, and re-layouts  9.49 us (1%)
    all_gather x2, waiting for transfers between devices, local(): whole_u = lax.all_gather(u_rows, 'fsdp', axis=0, tiled=True)  289 us
    all_gather x1, waiting for transfers between devices, local(): weight_piece = lax.all_gather(key_weight, 'fsdp', axis=0, tiled=True)  139 us
    all_gather x1, waiting for transfers between devices, local(): factor_piece = lax.all_gather(q_low, 'fsdp', axis=0, tiled=True)  107 us
    psum x1, blocking collectives, local(): sums = lax.psum(partial_sums, ('fsdp', 'seq'))  101 us
    all_gather x1, waiting for transfers between devices, local(): whole_x = lax.all_gather(tokens, 'seq', axis=1, tiled=True)[0]  88.4 us
    another operation x12, other arithmetic, solve_rows(): lower = jnp.linalg.cholesky(gram)  26.1 us
    dot_general x6, matrix products, highest(): jnp.dot(left, right, precision=lax.Precision.HIGHEST, preferred_element_t...  23.4 us
    another operation x8, other arithmetic, solve_rows(): lax.linalg.triangular_solve(lower, rows, left_side=False, lower=True, tra...  22.2 us
  transfers between devices with their start and end apart: 5, of which 5 were waited for; matrix products, arithmetic and copies ran while one was open for 4% of the time, Pallas kernels for 0%

commit v1 on v0

--- a/solution.py
+++ b/solution.py
@@ -30,7 +30,9 @@
         whole_u = lax.all_gather(u_rows, "fsdp", axis=0, tiled=True)
         u_rows = solve_rows(u_rows, highest(whole_u.T, whole_u))
     q_low = u_rows.astype(jnp.bfloat16)
-    whole_x = lax.all_gather(tokens, "seq", axis=1, tiled=True)[0]
+    whole_x = jnp.concatenate(
+        lax.all_to_all(jnp.stack([tokens] * lax.axis_size("seq")), "seq", 0, 0), axis=1
+    )[0]
     length = whole_x.shape[0]
     slice_width = key_weight.shape[1]
     weight_piece = lax.all_gather(key_weight, "fsdp", axis=0, tiled=True)

time: 859 us -> 765 us (0.89)
  waiting for transfers between devices: 625 us -> 521 us
    all_gather x1 -> x0, waiting for transfers between devices: 88.4 us -> none  [local(): whole_x = lax.all_gather(tokens, 'seq', axis=1, tiled=True)[0]]
    all_gather x1, waiting for transfers between devices: 107 us -> 32.4 us  [local(): factor_piece = lax.all_gather(q_low, 'fsdp', axis=0, tiled=True)]
    all_to_all x0 -> x1, waiting for transfers between devices: none -> 64.9 us  [local(): lax.all_to_all(jnp.stack([tokens] * lax.axis_size('seq')), 'seq', 0, 0)]
  transfers between devices with their start and end apart: 5 -> 5, of which waited for: 5 -> 5; matrix products, arithmetic and copies ran while one was open for 4% -> 5% of each run, Pallas kernels for 0% -> 0%
where the time goes in v1:
time: 765 us
  waiting for transfers between devices  521 us (68%)
  blocking collectives  101 us (13%)
  other arithmetic  60.2 us (8%)
  matrix products  47.1 us (6%)
  between operations  14 us (2%)
  local copies, waits for them, and re-layouts  13.6 us (2%)
    all_gather x2, waiting for transfers between devices, local(): whole_u = lax.all_gather(u_rows, 'fsdp', axis=0, tiled=True)  289 us
    all_gather x1, waiting for transfers between devices, local(): weight_piece = lax.all_gather(key_weight, 'fsdp', axis=0, tiled=True)  134 us
    psum x1, blocking collectives, local(): sums = lax.psum(partial_sums, ('fsdp', 'seq'))  101 us
    all_to_all x1, waiting for transfers between devices, local(): lax.all_to_all(jnp.stack([tokens] * lax.axis_size('seq')), 'seq', 0, 0)  64.9 us
    all_gather x1, waiting for transfers between devices, local(): factor_piece = lax.all_gather(q_low, 'fsdp', axis=0, tiled=True)  32.4 us
    another operation x12, other arithmetic, solve_rows(): lower = jnp.linalg.cholesky(gram)  26.1 us
    dot_general x6, matrix products, highest(): jnp.dot(left, right, precision=lax.Precision.HIGHEST, preferred_element_t...  23.3 us
    another operation x8, other arithmetic, solve_rows(): lax.linalg.triangular_solve(lower, rows, left_side=False, lower=True, tra...  22.2 us
  transfers between devices with their start and end apart: 5, of which 5 were waited for; matrix products, arithmetic and copies ran while one was open for 5% of the time, Pallas kernels for 0%

profile of v1, /device:TPU:1, one launch (start us, length us, event | category | flops | bytes accessed | tf_op | source)
XLA Modules:
  0.0 764.6 jit_solution(9688253466576569146)
XLA Ops:
  7.2 0.7 all-gather.5.cloned.1.call-update
  8.0 151.0 %all-gather.5.cloned.1.call-done = f32[8192,64]{1,0:T(8,128)} async-done(((f32[64,64]{1,0:T(8,128)}), f32[8192,64]{1,0:T(8,128)}) %all-gather.5.cloned.1.call-update) | async-done | bytes 2097168 | tf_op jit(solution)/shard_map/all_gather | solution.py:30
  159.0 10.4 %fusion.26 = f32[64,64]{1,0:T(8,128)S(1)} fusion(f32[8192,64]{1,0:T(8,128)} %all-gather.5.cloned.1.call-done), kind=kOutput, calls=%fused_computation.59 | convolution fusion | flops 402653184 | bytes 2113536 | tf_op jit(solution)/shard_map/dot_general | solution.py:16
  169.5 5.8 cholesky.74
  176.7 4.9 custom-call.10
  181.9 0.7 copy.22
  182.8 137.7 %all-gather.7.cloned.1.call-done = f32[8192,64]{1,0:T(8,128)} async-done(((f32[64,64]{1,0:T(8,128)}), f32[8192,64]{1,0:T(8,128)}) %all-gather.7.cloned.1.call-update) | async-done | bytes 2097168 | tf_op jit(solution)/shard_map/all_gather | solution.py:30
  320.6 10.4 %fusion.27 = f32[64,64]{1,0:T(8,128)S(1)} fusion(f32[8192,64]{1,0:T(8,128)} %all-gather.7.cloned.1.call-done), kind=kOutput, calls=%fused_computation.60 | convolution fusion | flops 402653184 | bytes 2113536 | tf_op jit(solution)/shard_map/dot_general | solution.py:16
  331.1 5.8 cholesky.85
  338.3 4.9 custom-call.11
  343.4 0.7 copy.27
  344.7 4.4 stack.16
  349.2 6.0 all-to-all-start
  355.7 5.8 cholesky.96
  362.8 4.9 custom-call.12
  368.6 5.8 cholesky.107
  375.8 4.9 custom-call.13
  380.7 2.5 copy.26
  383.7 64.9 %all-to-all-done = bf16[4,1,128,8192]{3,2,1,0:T(8,128)(2,1)} async-done(((bf16[4,1,128,8192]{3,2,1,0:T(8,128)(2,1)}), bf16[4,1,128,8192]{3,2,1,0:T(8,128)(2,1)}, u32[]{:S(2)}, u32[]{:S(2)}) %all-to-all-start) | async-done | bytes 8388640 | tf_op jit(solution)/shard_map/all_to_all | solution.py:34
  448.6 32.4 %all-gather.11.cloned.1.call-done = bf16[8192,64]{1,0:T(8,128)(2,1)} async-done(((bf16[64,64]{1,0:T(8,128)(2,1)}), bf16[8192,64]{1,0:T(8,128)(2,1)}) %all-gather.11.cloned.1.call-update) | async-done | bytes 1048592 | tf_op jit(solution)/shard_map/all_gather | solution.py:39
  481.0 6.7 fusion.30
  488.3 134.1 %all-gather.9.cloned.1.call-done = bf16[8192,256]{1,0:T(8,128)(2,1)} async-done(((bf16[64,256]{1,0:T(8,128)(2,1)}), bf16[8192,256]{1,0:T(8,128)(2,1)}) %all-gather.9.cloned.1.call-update) | async-done | bytes 4194320 | tf_op jit(solution)/shard_map/all_gather | solution.py:38
  622.4 6.9 add_convert_fusion
  629.8 25.2 %while.26 = (s32[]{:T(128)}, f32[2,2]{1,0:T(2,128)S(1)}, bf16[2,8,512,128]{2,3,1,0:T(8,128)(2,1)}, bf16[2,2,512,128]{3,2,1,0:T(8,128)(2,1)S(1)}, s32[]{:T(128)},...) while((s32[]{:T(128)}, f32[2,2]{1,0:T(2,128)S(1)}, ...), condition=%wide.region_9.13_spmd.clone.clone, body=%wide.region_2.12_spmd.clone.clone.sunk | while | flops 138674192 | bytes 10113394 | solution.py:70
  629.8 1.3 constant_dynamic-slice_fusion.2
  631.1 0.7 copy.33
  631.9 10.4 %while.27 = (s32[]{:T(128)}, f32[8,2]{1,0:T(8,128)S(1)}, pred[512,512]{0,1:T(8,128)(4,1)S(1)}, bf16[8,512,128]{2,1,0:T(8,128)(2,1)S(1)}, bf16[2,512,128]{2,1,0:T(8,128)(2,1)S(1)}, /*index=5*/s32[]{:T(128)}, s32[]{:T(128)}) while((s32[]{:T(128)}, f32[8,2]{1,0:T(8,128)S(1)}, pred[512,512]{0,1:T(8,128)(4,1)S(1)}, ...), condition=%wide.region_7.10_spmd.clone, body=%wide.region_3.9_spmd.clone.sunk | while | flops 138412032 | bytes 5132397 | solution.py:67
  642.4 1.3 constant_dynamic-slice_fusion.2
  643.7 0.7 copy.33
  644.5 10.4 %while.27 = (s32[]{:T(128)}, f32[8,2]{1,0:T(8,128)S(1)}, pred[512,512]{0,1:T(8,128)(4,1)S(1)}, bf16[8,512,128]{2,1,0:T(8,128)(2,1)S(1)}, bf16[2,512,128]{2,1,0:T(8,128)(2,1)S(1)}, /*index=5*/s32[]{:T(128)}, s32[]{:T(128)}) while((s32[]{:T(128)}, f32[8,2]{1,0:T(8,128)S(1)}, pred[512,512]{0,1:T(8,128)(4,1)S(1)}, ...), condition=%wide.region_7.10_spmd.clone, body=%wide.region_3.9_spmd.clone.sunk | while | flops 138412032 | bytes 5132397 | solution.py:67
  655.0 1.1 convolution_multiply_fusion.1
  656.1 101.5 %psum.7 = f32[2]{0:T(128)S(1)} all-reduce(f32[2]{0:T(128)S(1)} %reduce_sum.36), channel_id=1, replica_groups=mesh['fsdp'=128,'seq'=4] {'fsdp','seq'}, use_global_device_ids=true, to_apply=%region_11.15 | all-reduce | flops 2 | bytes 16 | tf_op jit(solution)/shard_map/psum | solution.py:71
  (122 shorter events, 31.0 us)
Async XLA Ops:
  7.2 348.0 %copy-start = (f32[1024,64]{0,1:T(8,128)S(1)}, f32[1024,64]{0,1:T(8,128)}, u32[]{:S(2)}) copy-start(f32[1024,64]{0,1:T(8,128)} %param.18) | copy-start | bytes 786436
  7.2 151.8 %all-gather.5.cloned.1.call-start = ((), (), s32[]{:S(2)}) async-start(), calls=%async_computation.1 | async-start | bytes 4227072 | tf_op jit(solution)/shard_map/all_gather | solution.py:30
  7.9 173.7 %copy-start.3 = (f32[64,64]{1,0:T(8,128)S(1)}, f32[64,64]{1,0:T(8,128)}, u32[]{:S(2)}) copy-start(f32[64,64]{1,0:T(8,128)} %param.17) | copy-start | bytes 49156
  7.9 312.6 %all-gather.7.cloned.1.call-start = ((), (), s32[]{:S(2)}) async-start(), calls=%async_computation.2 | async-start | bytes 4227072 | tf_op jit(solution)/shard_map/all_gather | solution.py:30
  182.6 162.1 %copy-start.1 = (bf16[1,128,8192]{2,1,0:T(8,128)(2,1)S(1)}, bf16[1,128,8192]{2,1,0:T(8,128)(2,1)}, u32[]{:S(2)}) copy-start(bf16[1,128,8192]{2,1,0:T(8,128)(2,1)} %param.14) | copy-start | bytes 6291460
  182.6 298.4 %all-gather.11.cloned.1.call-start = ((), (), s32[]{:S(2)}) async-start(), calls=%async_computation.4 | async-start | bytes 2113536 | tf_op jit(solution)/shard_map/all_gather | solution.py:39
  344.2 278.2 %all-gather.9.cloned.1.call-start = ((), (), s32[]{:S(2)}) async-start(), calls=%async_computation.3 | async-start | bytes 4227072 | tf_op jit(solution)/shard_map/all_gather | solution.py:38
  349.2 31.6 %copy-start.2 = (bf16[1,512,2048]{2,1,0:T(8,128)(2,1)S(1)}, bf16[1,512,2048]{2,1,0:T(8,128)(2,1)}, u32[]{:S(2)}) copy-start(bf16[1,512,2048]{2,1,0:T(8,128)(2,1)} %param.15) | copy-start | bytes 6291460
  349.2 99.4 %all-to-all-start = ((bf16[4,1,128,8192]{3,2,1,0:T(8,128)(2,1)}), bf16[4,1,128,8192]{3,2,1,0:T(8,128)(2,1)}, u32[]{:S(2)}, u32[]{:S(2)}) async-start(bf16[4,1,128,8192]{3,2,1,0:T(8,128)(2,1)} %stack.16), calls=%async_computation | async-start | bytes 16777216 | tf_op jit(solution)/shard_map/all_to_all | solution.py:34
Sparse Core Ops, SparseCore 0:
  11.1 147.8 all-gather.4
  182.7 137.7 all-gather.6
  344.3 136.6 all-gather.10
  484.0 138.3 all-gather.8
